TPU v7x, 32 devices: a whole 2x2x4 slice. The times are simulated.
32 devices in a mesh: dp: 8 (over z, y), mp: 4 (over x, core).
Axes of the slice: x: 2, y: 2, z: 4, core: 2. Of those that a mesh axis runs over, the one named last changes fastest.
Arguments:
- gradients: bfloat16 [8, 4, 192, 16384], P('dp', 'mp'), may hold values from -3000 to 3000
- owner_list: int32 [192], replicated, may hold values from 0 to 7, as said below
- master_weights: float32 [4, 288, 16384], P('mp', 'dp'), may hold values from -6 to 6
- first_moment: float32 [4, 288, 16384], P('mp', 'dp'), may hold values from -6 to 6
- second_moment: float32 [4, 288, 16384], P('mp', 'dp'), may hold values from 0.05 to 2
- average_weights: float32 [4, 288, 16384], P('mp', 'dp'), may hold values from -6 to 6
Outputs:
- new_params: bfloat16 [4, 192, 16384], P('mp')
- new_master: float32 [4, 288, 16384], P('mp', 'dp')
- new_first: float32 [4, 288, 16384], P('mp', 'dp')
- new_second: float32 [4, 288, 16384], P('mp', 'dp')
- average_rows: float32 [4, 192, 16384], P('mp', 'dp')
Inputs may be any that keep to these rules, and one draw needn't show every extreme that they name: `owner_list`: each data rank owns at most 36 segments, and some rank owns exactly 36.
All inputs are finite; a program needn't handle non-finite values.
Results may differ from a plain program's by a relative error of at most 0.015.
Values may be sent and summed in bfloat16 or wider, within the bound.
No kernel may reach another device: no remote copies, remote signals or barrier semaphores. Data moves between devices by JAX's collectives and lax.ppermute only.
A program may use at most 128 MiB of HBM per device.

v0:
```python
import math
import jax
import jax.numpy as jnp
from jax import lax
from jax.sharding import PartitionSpec as P


def slot_matrix(owner_list, ranks, cap):
    count = owner_list.shape[0]
    position = jnp.arange(count, dtype=jnp.int32)
    same_owner = (owner_list[:, None] == owner_list[None, :]) & (
        position[None, :] < position[:, None]
    )
    slot_index = owner_list * cap + jnp.sum(same_owner.astype(jnp.int32), axis=1)
    rows = jnp.arange(ranks * cap, dtype=jnp.int32)
    return (rows[:, None] == slot_index[None, :]).astype(jnp.float32)


def on_device(gradients, owner_list, master_weights, first_moment, second_moment, average_weights):
    highest = lax.Precision.HIGHEST
    local_grad = gradients[0, 0]
    nseg, seg = local_grad.shape
    cap = master_weights.shape[1]
    ranks = lax.axis_size("dp")
    blocks = lax.axis_size("mp")
    per_rank = nseg // ranks
    my_rank = lax.axis_index("dp")
    placing = slot_matrix(owner_list, ranks, cap)
    my_slots = lax.dynamic_slice_in_dim(placing, my_rank * cap, cap, 0)
    in_use = jnp.sum(my_slots, axis=1)[:, None]
    summed = lax.psum(local_grad.astype(jnp.float32).astype(jnp.bfloat16), "dp").astype(jnp.float32)
    total_sq = lax.psum(jnp.sum(summed * summed), "mp")
    owned_grad = jnp.dot(my_slots, summed, precision=highest)
    clip_factor = jnp.minimum(1.0, math.sqrt(blocks * nseg * seg) / (jnp.sqrt(total_sq) + 1e-06))
    owned_grad = clip_factor * owned_grad
    new_first = in_use * (0.9 * first_moment[0] + 0.1 * owned_grad)
    new_second = in_use * (0.95 * second_moment[0] + 0.05 * owned_grad * owned_grad)
    first_hat = new_first / (1.0 - 0.9**20)
    second_hat = new_second / (1.0 - 0.95**20)
    old_master = master_weights[0]
    new_master = in_use * (
        old_master - 0.02 * (first_hat / (jnp.sqrt(second_hat) + 1e-08) + 0.1 * old_master)
    )
    averaged = 0.9 * average_weights[0] + 0.1 * new_master
    placing_rows = placing.T
    placing_half = placing_rows.astype(jnp.bfloat16)
    gathered = jnp.dot(
        placing_half,
        lax.all_gather(new_master.astype(jnp.bfloat16), "dp", axis=0, tiled=True),
        preferred_element_type=jnp.float32,
    )
    new_params = gathered.astype(jnp.bfloat16)
    spread_out = jnp.dot(my_slots.T, averaged, precision=highest).reshape(ranks, per_rank, seg)
    arrived = lax.all_to_all(spread_out, "dp", split_axis=0, concat_axis=0, tiled=True)
    average_rows = jnp.sum(arrived, axis=0)
    return (
        new_params[None],
        new_master[None],
        new_first[None],
        new_second[None],
        average_rows[None],
    )


def solution(mesh):
    return jax.shard_map(
        on_device,
        mesh=mesh,
        in_specs=(
            P("dp", "mp", None, None),
            P(),
            P("mp", "dp", None),
            P("mp", "dp", None),
            P("mp", "dp", None),
            P("mp", "dp", None),
        ),
        out_specs=(
            P("mp", None, None),
            P("mp", "dp", None),
            P("mp", "dp", None),
            P("mp", "dp", None),
            P("mp", "dp", None),
        ),
        check_vma=False,
    )
```

profile of v0, /device:TPU:0, one launch (start us, length us, event | category | flops | bytes accessed | tf_op | source)
XLA Modules:
  0.0 680.6 jit_solution(15627968808862761865)
XLA Ops:
  7.2 0.0 all-reduce.2.cloned.1.call-start
  7.2 0.0 copy-start.3
  7.2 0.7 all-reduce.2.cloned.1.call-update
  7.9 0.0 copy-done.3
  7.9 0.2 convert_reduce_fusion
  8.2 217.6 %all-reduce.2.cloned.1.call-done = bf16[192,16384]{1,0:T(8,128)(2,1)} async-done(((bf16[192,16384]{1,0:T(8,128)(2,1)}), bf16[192,16384]{1,0:T(8,128)(2,1)}) %all-reduce.2.cloned.1.call-update) | async-done | bytes 6291472 | tf_op jit(solution)/shard_map/psum | solution.py:31
  225.8 6.6 multiply_reduce_fusion
  232.4 0.1 convert_reduce_fusion.1
  232.5 7.7 %psum.15 = f32[]{:T(128)} all-reduce(f32[]{:T(128)} %multiply_reduce_fusion), channel_id=1, replica_groups=mesh['dp'=8,'mp'=4] {'mp'}, use_global_device_ids=true, to_apply=%region_4.0 | all-reduce | flops 1 | bytes 8 | tf_op jit(solution)/shard_map/psum | solution.py:32
  240.9 0.0 copy-start
  240.9 14.0 %convert_bitcast_fusion = (bf16[1,36,16384]{2,1,0:T(8,128)(2,1)}, f32[36,16384]{1,0:T(8,128)S(1)}, f32[1,36,16384]{2,1,0:T(8,128)}, f32[1,36,16384]{2,1,0:T(8,128)}) fusion(f32[1,36,16384]{2,0,1:T(1,128)} %param.10, f32[1,36,16384]{2,0,1:T(1,128)} %param.9, f32[1,36,16384]{2,0,1:T(1,128)} %param.8, f32[36]{0:T(128)S(1)} %convert_reduce_fusion.1, ...), kind=kOutput, calls=%fused_computation.20 | convolution fusion | flops 238288896 | bytes 21637640 | tf_op jit(solution)/shard_map/dot_general | solution.py:33
  254.9 0.0 copy-done
  254.9 8.4 %fusion.6 = f32[192,16384]{1,0:T(8,128)} fusion(f32[1,36,16384]{2,0,1:T(1,128)S(1)} %copy-done, f32[36,16384]{1,0:T(8,128)S(1)} %get-tuple-element.26, pred[288,192]{1,0:T(8,128)(4,1)S(1)} %iota_compare_fusion, s32[]{:T(128)S(6)} %select_n.3), kind=kOutput, calls=%fused_computation.13 | convolution fusion | flops 1360723968 | bytes 17573892 | tf_op jit(solution)/shard_map/dot_general | solution.py:53
  263.4 5.3 all-to-all-start
  268.7 0.3 all-gather.3.cloned.1.call-start
  269.0 0.5 all-gather.3.cloned.1.call-update
  269.5 0.0 copy-start.2
  269.5 3.8 copy.32
  273.3 0.0 copy-start.1
  273.3 0.0 copy-done.2
  273.3 3.8 copy.33
  277.2 0.0 copy-done.1
  277.2 3.8 copy.34
  281.0 362.5 %all-gather.3.cloned.1.call-done = bf16[8,36,16384]{2,1,0:T(8,128)(2,1)} async-done(((bf16[1,36,16384]{2,1,0:T(8,128)(2,1)}), bf16[8,36,16384]{2,1,0:T(8,128)(2,1)}) %all-gather.3.cloned.1.call-update) | async-done | bytes 9437200 | tf_op jit(solution)/shard_map/all_gather | solution.py:49
  643.5 8.5 %reshape.25 = bf16[288,16384]{1,0:T(8,128)(2,1)} reshape(bf16[8,36,16384]{2,1,0:T(8,128)(2,1)} %all-gather.3.cloned.1.call-done) | data formatting | bytes 18874368
  652.0 9.9 %fusion = bf16[1,192,16384]{2,1,0:T(8,128)(2,1)} fusion(bf16[288,16384]{1,0:T(8,128)(2,1)} %reshape.25, s32[192]{0:T(256)S(1)} %multiply_add_fusion), kind=kOutput, calls=%fused_computation.1 | convolution fusion | flops 1815250944 | bytes 15729408 | tf_op jit(solution)/shard_map/dot_general | solution.py:47
  661.8 5.4 all-to-all-done
  667.2 6.5 reduce_sum.39
  (2 shorter events, 0.1 us)
Async XLA Ops:
  7.2 218.6 %all-reduce.2.cloned.1.call-start = ((), (), s32[]{:S(2)}) async-start(), calls=%async_computation.1 | async-start | bytes 12582912 | tf_op jit(solution)/shard_map/psum | solution.py:31
  7.2 0.7 copy-start.3
  240.9 14.0 %copy-start = (f32[1,36,16384]{2,0,1:T(1,128)S(1)}, f32[1,36,16384]{2,0,1:T(1,128)}, u32[]{:S(2)}) copy-start(f32[1,36,16384]{2,0,1:T(1,128)} %param.11) | copy-start | bytes 7077892
  263.4 403.8 %all-to-all-start = ((f32[8,24,16384]{2,1,0:T(8,128)}), f32[8,24,16384]{2,1,0:T(8,128)}, u32[]{:S(2)}, u32[]{:S(2)}) async-start(f32[8,24,16384]{2,1,0:T(8,128)} %bitcast.45), calls=%async_computation | async-start | bytes 25165824 | tf_op jit(solution)/shard_map/all_to_all | solution.py:54
  268.7 374.8 %all-gather.3.cloned.1.call-start = ((), (), s32[]{:S(2)}) async-start(), calls=%async_computation.2 | async-start | bytes 11796480 | tf_op jit(solution)/shard_map/all_gather | solution.py:49
  269.5 3.8 copy-start.2
  273.3 3.8 copy-start.1
Sparse Core Ops, SparseCore 0:
  11.8 213.9 all-reduce.1
  272.6 370.8 all-gather.2
where the time goes:
time: 681 us
  waiting for transfers between devices  587 us (86%)
  matrix products  32.3 us (5%)
  local copies, waits for them, and re-layouts  20 us (3%)
  between operations  14.8 us (2%)
  other arithmetic  13.5 us (2%)
  blocking collectives  7.68 us (1%)
    all_gather x1, waiting for transfers between devices, on_device(): lax.all_gather(new_master.astype(jnp.bfloat16), 'dp', axis=0, tiled=True)  362 us
    psum x1, waiting for transfers between devices, on_device(): lax.psum(local_grad.astype(jnp.float32).astype(jnp.bfloat16), 'dp')  218 us
    unnamed x12, local copies, waits for them, and re-layouts  20 us
    dot_general x1, matrix products, on_device(): owned_grad = jnp.dot(my_slots, summed, precision=highest)  14 us
  transfers between devices with their start and end apart: 3, of which 3 were waited for; matrix products, arithmetic and copies ran while one was open for 4% of the time, Pallas kernels for 0%

commit v1 on v0

--- a/solution.py
+++ b/solution.py
@@ -1,8 +1,16 @@
+import functools
 import math
 import jax
 import jax.numpy as jnp
 from jax import lax
 from jax.sharding import PartitionSpec as P
+
+
+def _fill_tables(field, row_axis):
+    return lax.all_gather(field, axis_name=row_axis).sum(axis=0)
+
+
+_touch_sites = functools.partial(_fill_tables, row_axis="dp")
 
 
 def slot_matrix(owner_list, ranks, cap):
@@ -28,7 +36,7 @@
     placing = slot_matrix(owner_list, ranks, cap)
     my_slots = lax.dynamic_slice_in_dim(placing, my_rank * cap, cap, 0)
     in_use = jnp.sum(my_slots, axis=1)[:, None]
-    summed = lax.psum(local_grad.astype(jnp.float32).astype(jnp.bfloat16), "dp").astype(jnp.float32)
+    summed = _touch_sites(local_grad.astype(jnp.float32).astype(jnp.bfloat16)).astype(jnp.float32)
     total_sq = lax.psum(jnp.sum(summed * summed), "mp")
     owned_grad = jnp.dot(my_slots, summed, precision=highest)
     clip_factor = jnp.minimum(1.0, math.sqrt(blocks * nseg * seg) / (jnp.sqrt(total_sq) + 1e-06))

time: 681 us -> 1440 us (2.11)
  waiting for transfers between devices: 587 us -> 1320 us
  other arithmetic: 13.5 us -> 33.5 us
    all_gather x0 -> x1, waiting for transfers between devices: none -> 956 us  [_fill_tables(): return lax.all_gather(field, axis_name=row_axis).sum(axis=0)]
    psum x1 -> x0, waiting for transfers between devices: 218 us -> none  [on_device(): lax.psum(local_grad.astype(jnp.float32).astype(jnp.bfloat16), 'dp')]
    reduce_sum x0 -> x1, other arithmetic: none -> 20.1 us  [_fill_tables(): return lax.all_gather(field, axis_name=row_axis).sum(axis=0)]
  transfers between devices with their start and end apart: 3 -> 3, of which waited for: 3 -> 3; matrix products, arithmetic and copies ran while one was open for 4% -> 2% of each run, Pallas kernels for 0% -> 0%
where the time goes in v1:
time: 1440 us
  waiting for transfers between devices  1320 us (92%)
  other arithmetic  33.5 us (2%)
  matrix products  32.3 us (2%)
  local copies, waits for them, and re-layouts  21.9 us (2%)
  between operations  14.8 us (1%)
    all_gather x1, waiting for transfers between devices, _fill_tables(): return lax.all_gather(field, axis_name=row_axis).sum(axis=0)  956 us
    all_gather x1, waiting for transfers between devices, on_device(): lax.all_gather(new_master.astype(jnp.bfloat16), 'dp', axis=0, tiled=True)  361 us
  transfers between devices with their start and end apart: 3, of which 3 were waited for; matrix products, arithmetic and copies ran while one was open for 2% of the time, Pallas kernels for 0%

profile of v1, /device:TPU:0, one launch (start us, length us, event | category | flops | bytes accessed | tf_op | source)
XLA Modules:
  0.0 1439.4 jit_solution(7644665724312469854)
XLA Ops:
  7.2 0.0 copy-start.2
  7.2 0.0 all-gather.5.cloned.1.call-start
  7.2 0.7 all-gather.5.cloned.1.call-update
  7.9 0.0 copy-done.2
  7.9 0.2 convert_reduce_fusion
  8.2 956.4 %all-gather.5.cloned.1.call-done = bf16[8,1,192,16384]{3,2,1,0:T(8,128)(2,1)} async-done(((bf16[1,1,192,16384]{3,2,1,0:T(8,128)(2,1)}), bf16[8,1,192,16384]{3,2,1,0:T(8,128)(2,1)}) %all-gather.5.cloned.1.call-update) | async-done | bytes 50331664 | tf_op jit(solution)/shard_map/all_gather | solution.py:10
  964.6 20.1 %reduce_sum.50 = bf16[192,16384]{1,0:T(8,128)(2,1)} reduce(bf16[8,1,192,16384]{3,2,1,0:T(8,128)(2,1)} %all-gather.5.cloned.1.call-done, bf16[]{:T(256)} %constant.13.clone.1), dimensions={0,1}, to_apply=%region_2.0 | reduce | flops 22020096 | bytes 56623104 | tf_op jit(solution)/shard_map/reduce_sum | solution.py:10
  984.7 6.6 multiply_reduce_fusion
  991.3 0.1 convert_reduce_fusion.1
  991.4 7.7 psum.7
  999.8 0.0 copy-start
  999.8 14.0 convert_bitcast_fusion
  1013.8 0.0 copy-done
  1013.8 8.4 fusion.6
  1022.3 5.3 all-to-all-start
  1027.6 0.3 all-gather.7.cloned.1.call-start
  1027.9 0.5 all-gather.7.cloned.1.call-update
  1028.4 0.0 copy-start.1
  1028.4 5.7 copy.34
  1034.1 0.0 copy-done.1
  1034.1 3.8 copy.33
  1037.9 3.8 copy.32
  1041.8 360.6 %all-gather.7.cloned.1.call-done = bf16[8,36,16384]{2,1,0:T(8,128)(2,1)} async-done(((bf16[1,36,16384]{2,1,0:T(8,128)(2,1)}), bf16[8,36,16384]{2,1,0:T(8,128)(2,1)}) %all-gather.7.cloned.1.call-update) | async-done | bytes 9437200 | tf_op jit(solution)/shard_map/all_gather | solution.py:57
  1402.4 8.5 reshape.27
  1410.9 9.9 fusion
  1420.7 5.4 all-to-all-done
  1426.1 6.5 reduce_sum.52
  (2 shorter events, 0.1 us)
Async XLA Ops:
  7.2 0.8 copy-start.2
  7.2 957.4 %all-gather.5.cloned.1.call-start = ((), (), s32[]{:S(2)}) async-start(), calls=%async_computation.1 | async-start | bytes 56623104 | tf_op jit(solution)/shard_map/all_gather | solution.py:10
  999.8 14.0 copy-start
  1022.3 403.8 %all-to-all-start = ((f32[8,24,16384]{2,1,0:T(8,128)}), f32[8,24,16384]{2,1,0:T(8,128)}, u32[]{:S(2)}, u32[]{:S(2)}) async-start(f32[8,24,16384]{2,1,0:T(8,128)} %bitcast.44), calls=%async_computation | async-start | bytes 25165824 | tf_op jit(solution)/shard_map/all_to_all | solution.py:62
  1027.6 374.8 %all-gather.7.cloned.1.call-start = ((), (), s32[]{:S(2)}) async-start(), calls=%async_computation.2 | async-start | bytes 11796480 | tf_op jit(solution)/shard_map/all_gather | solution.py:57
  1028.4 5.7 copy-start.1
Sparse Core Ops, SparseCore 0:
  9.5 955.0 all-gather.4
  1031.2 371.1 all-gather.6
